TPU v7x, 32 devices: a whole 2x2x4 slice. The times are simulated.
32 devices in a mesh: req: 2 (over x), ctx: 8 (over z, core), exp: 2 (over y).
Axes of the slice: x: 2, y: 2, z: 4, core: 2. Of those that a mesh axis runs over, the one named last changes fastest.
Arguments:
- query_states: bfloat16 [2, 512, 1024], P('req', 'ctx', 'exp'), may hold values from -6 to 6
- key_states: bfloat16 [2, 512, 1024], P('req', 'ctx', 'exp'), may hold values from -6 to 6
- value_states: bfloat16 [2, 512, 1024], P('req', 'ctx', 'exp'), may hold values from -6 to 6
- residual: bfloat16 [2, 512, 2048], P('req', ('ctx', 'exp')), may hold values from -6 to 6
- out_weight: bfloat16 [2048, 1024], P('ctx', 'exp'), may hold values from -0.1875 to 0.1875
- norm_gain: float32 [2048], replicated, may hold values from 0.1 to 1.9
- gate_weight: bfloat16 [8, 2048, 704], P('ctx', None, 'exp'), may hold values from -0.125 to 0.125
- up_weight: bfloat16 [8, 2048, 704], P('ctx', None, 'exp'), may hold values from -0.125 to 0.125
- down_weight: bfloat16 [8, 704, 2048], P('ctx', 'exp'), may hold values from -0.21875 to 0.21875
- routes: int32 [2, 512, 4], P('req', 'ctx'), may hold values from 0 to 7, all different within a row; in each aligned block of 64 rows (0 to 63, 64 to 127, ..., all dimensions but the last counted through in order) at most 48 rows name the same one
- route_weights: float32 [2, 512, 4], P('req', 'ctx'), may hold values from 0.1 to 1
- prompt_lengths: int32 [2], P('req'), may hold values from 128 to 512, as said below
Outputs:
- layer_out: bfloat16 [2, 512, 2048], P('req', ('ctx', 'exp'))
- cache_keys: bfloat16 [2, 512, 1024], P('req', 'ctx', 'exp')
- cache_values: bfloat16 [2, 512, 1024], P('req', 'ctx', 'exp')
Inputs may be any that keep to these rules, and one draw needn't show every extreme that they name: `routes`: each row names 4 different experts; in each aligned block of 64 rows of a request no expert is named by more than 48 rows, a bound that some block reaches. `prompt_lengths`: one request has exactly 512 tokens.
All inputs are finite; a program needn't handle non-finite values.
Results may differ from a plain program's by a relative error of at most 0.019.
Values may be sent and summed in bfloat16 or wider, within the bound.
No kernel may reach another device: no remote copies, remote signals or barrier semaphores. Data moves between devices by JAX's collectives and lax.ppermute only.
A program may use at most 64 MiB of HBM per device.

v0:
```python
import jax
import jax.numpy as jnp
from jax import lax
from jax.sharding import PartitionSpec as P

D = 2048
HD = 128
TOP = 4
EPS = 1e-06
NEG = -1e30


def row_positions(row_ids, half_block, n_groups):
    block_ids = row_ids // half_block
    device = block_ids // 2
    target = jnp.where(block_ids % 2 == 0, device, 2 * n_groups - 1 - device)
    return target * half_block + row_ids % half_block


def slot_tables(route_block, weight_block, experts, capacity):
    tok_here, top_here = route_block.shape
    flat_ids = route_block.reshape(tok_here * top_here)
    hit_table = (flat_ids[:, None] == jnp.arange(experts, dtype=jnp.int32)[None, :]).astype(
        jnp.int32
    )
    before = jnp.cumsum(hit_table, axis=0) - hit_table
    slot_rank = jnp.sum(before * hit_table, axis=1)
    slot_index = flat_ids * capacity + slot_rank
    slot_match = (
        jnp.arange(experts * capacity, dtype=jnp.int32)[:, None] == slot_index[None, :]
    ).astype(jnp.float32)
    slot_match = slot_match.reshape(experts * capacity, tok_here, top_here)
    dispatch = jnp.sum(slot_match, axis=2)
    combine = jnp.transpose(jnp.sum(slot_match * weight_block[None, :, :], axis=2))
    return (dispatch, combine)


def expert_ffn(token_rows, gate_matrix, up_matrix, down_matrix):
    gate_act = jnp.dot(token_rows, gate_matrix, preferred_element_type=jnp.float32)
    up_act = jnp.dot(token_rows, up_matrix, preferred_element_type=jnp.float32)
    hidden = (jax.nn.silu(gate_act) * up_act).astype(jnp.bfloat16)
    return jnp.dot(hidden, down_matrix, preferred_element_type=jnp.float32)


def exp_swap(x):
    return lax.ppermute(x, "exp", perm=[(0, 1), (1, 0)])


def exp_reduce_rows(parts):
    if lax.axis_size("exp") != 2:
        return lax.psum_scatter(
            parts.astype(jnp.bfloat16), "exp", scatter_dimension=0, tiled=True
        ).astype(jnp.float32)
    half = parts.shape[0] // 2
    first = lax.axis_index("exp") == 0
    lower = parts[:half]
    upper = parts[half:]
    mine = jnp.where(first, lower, upper)
    theirs = jnp.where(first, upper, lower)
    got = exp_swap(theirs.astype(jnp.bfloat16))
    return mine + got.astype(jnp.float32)


def exp_gather_rows(rows):
    if lax.axis_size("exp") != 2:
        return lax.all_gather(rows, "exp", axis=0, tiled=True)
    got = exp_swap(rows)
    first = lax.axis_index("exp") == 0
    return jnp.where(
        first, jnp.concatenate([rows, got], axis=0), jnp.concatenate([got, rows], axis=0)
    )


def local(
    query_states,
    key_states,
    value_states,
    residual,
    out_weight,
    norm_gain,
    gate_weight,
    up_weight,
    down_weight,
    routes,
    route_weights,
    prompt_lengths,
):
    n_ctx = lax.axis_size("ctx")
    my_ctx = lax.axis_index("ctx")
    tok_here = query_states.shape[1]
    feat_width = query_states.shape[2]
    heads_dev = feat_width // HD
    half_block = tok_here // 2
    score_scale = HD ** (-0.5)
    length = prompt_lengths[0]
    local_ids = jnp.arange(tok_here, dtype=jnp.int32)
    query_pos = row_positions(my_ctx * tok_here + local_ids, half_block, n_ctx)
    decode_pos = my_ctx * tok_here + local_ids
    query_three = query_states[0].reshape(tok_here, heads_dev, HD)
    run_max = jnp.full((heads_dev, tok_here), NEG, jnp.float32)
    kv_here = jnp.concatenate([key_states[0], value_states[0]], axis=1)
    kv_all = lax.all_gather(kv_here, "ctx", axis=0, tiled=True)
    key_two = kv_all[:, :feat_width]
    value_two = kv_all[:, feat_width:]
    row_count = key_two.shape[0]
    key_pos = row_positions(jnp.arange(row_count, dtype=jnp.int32), half_block, n_ctx)
    pick_rows = (decode_pos[:, None] == key_pos[None, :]).astype(jnp.bfloat16)
    kept_keys = jnp.dot(pick_rows, key_two, preferred_element_type=jnp.float32)
    kept_values = jnp.dot(pick_rows, value_two, preferred_element_type=jnp.float32)
    old_max = run_max
    key_heads = key_two.reshape(row_count, heads_dev, HD)
    value_heads = value_two.reshape(row_count, heads_dev, HD)
    logits = (
        jnp.einsum("qhd,khd->hqk", query_three, key_heads, preferred_element_type=jnp.float32)
        * score_scale
    )
    visible = (key_pos[None, :] <= query_pos[:, None]) & (key_pos[None, :] < length)
    logits = jnp.where(visible[None], logits, NEG)
    new_max = jnp.maximum(old_max, jnp.max(logits, axis=2))
    weights = jnp.where(visible[None], jnp.exp(logits - new_max[:, :, None]), 0.0)
    new_sum = jnp.sum(weights, axis=2)
    gained = jnp.einsum(
        "hqk,khd->hqd",
        weights.astype(jnp.bfloat16),
        value_heads,
        preferred_element_type=jnp.float32,
    )
    inner_state = (new_max, new_sum, gained)
    run_max, run_sum, run_out, kept_keys, kept_values = inner_state + (kept_keys, kept_values)
    mixed = (run_out / run_sum[:, :, None]).astype(jnp.bfloat16)
    mixed = jnp.transpose(mixed, (1, 0, 2)).reshape(tok_here, feat_width)
    out_parts = jnp.einsum(
        "tc,oc->to",
        mixed,
        lax.all_gather(out_weight, "ctx", axis=0, tiled=True),
        preferred_element_type=jnp.float32,
    )
    head_total = exp_reduce_rows(out_parts)
    stream = (residual[0].astype(jnp.float32) + head_total).astype(jnp.bfloat16)
    stream_f = stream.astype(jnp.float32)
    mean_sq = jnp.mean(stream_f * stream_f, axis=1, keepdims=True)
    normed = (stream_f * lax.rsqrt(mean_sq + EPS) * norm_gain).astype(jnp.bfloat16)
    all_normed = exp_gather_rows(normed)
    capacity = min(tok_here, 2 * max(1, 3 * tok_here * TOP // (4 * n_ctx)))
    dispatch, combine = slot_tables(routes[0], route_weights[0], n_ctx, capacity)
    send_rows = jnp.dot(
        dispatch.astype(jnp.bfloat16), all_normed, preferred_element_type=jnp.float32
    ).astype(jnp.bfloat16)
    send_rows = send_rows.reshape(n_ctx, capacity, D)
    arrived = lax.all_to_all(send_rows, "ctx", split_axis=0, concat_axis=0, tiled=True)
    slot_count = arrived.shape[1]
    flat_rows = arrived.reshape(n_ctx * slot_count, D)
    produced = expert_ffn(flat_rows, gate_weight[0], up_weight[0], down_weight[0]).reshape(
        n_ctx, slot_count, D
    )
    served = lax.all_to_all(
        produced.astype(jnp.bfloat16), "ctx", split_axis=0, concat_axis=0, tiled=True
    ).astype(produced.dtype)
    results = served.reshape(n_ctx * capacity, D)
    moe_part = jnp.dot(
        combine, results, precision=lax.Precision.HIGHEST, preferred_element_type=jnp.float32
    )
    moe_rows = exp_reduce_rows(moe_part)
    layer_out = (stream.astype(jnp.float32) + moe_rows).astype(jnp.bfloat16)
    return (
        layer_out[None],
        kept_keys.astype(jnp.bfloat16)[None],
        kept_values.astype(jnp.bfloat16)[None],
    )


def solution(mesh):
    return jax.shard_map(
        local,
        mesh=mesh,
        in_specs=(
            P("req", "ctx", "exp"),
            P("req", "ctx", "exp"),
            P("req", "ctx", "exp"),
            P("req", ("ctx", "exp"), None),
            P("ctx", "exp"),
            P(),
            P("ctx", None, "exp"),
            P("ctx", None, "exp"),
            P("ctx", "exp", None),
            P("req", "ctx", None),
            P("req", "ctx", None),
            P("req"),
        ),
        out_specs=(P("req", ("ctx", "exp"), None), P("req", "ctx", "exp"), P("req", "ctx", "exp")),
        check_vma=False,
    )
```

profile of v0, /device:TPU:0, one launch (start us, length us, event | category | flops | bytes accessed | tf_op | source)
XLA Modules:
  0.0 180.0 jit_solution(15707757264715683724)
XLA Ops:
  7.2 0.0 copy-start
  7.2 0.0 all-gather.3.cloned.1.call-start
  7.2 1.6 pad_maximum_fusion
  8.9 0.0 all-gather.3.cloned.1.call-update
  8.9 0.0 all-gather.5.cloned.1.call-start
  8.9 0.7 all-gather.5.cloned.1.call-update
  10.3 0.8 copy.47
  11.1 0.1 eq.92
  11.2 0.6 reduce-window.6
  11.8 0.9 reshape_squeeze.4
  12.7 0.1 compare_and_fusion
  12.8 22.2 %all-gather.3.cloned.1.call-done = bf16[512,1024]{1,0:T(8,128)(2,1)} async-done(((bf16[64,1024]{1,0:T(8,128)(2,1)}), bf16[512,1024]{1,0:T(8,128)(2,1)}) %all-gather.3.cloned.1.call-update) | async-done | bytes 1048592 | tf_op jit(solution)/shard_map/all_gather | solution.py:102
  35.0 1.3 fusion.71
  36.3 0.2 copy.54
  36.5 0.2 copy.55
  36.7 0.3 fusion.72
  37.1 0.2 fusion.18
  37.3 0.3 fusion.15
  37.7 0.0 copy-start.2
  37.7 0.0 copy-start.3
  37.7 27.7 %all-gather.5.cloned.1.call-done = bf16[2048,512]{1,0:T(8,128)(2,1)} async-done(((bf16[256,512]{1,0:T(8,128)(2,1)}), bf16[2048,512]{1,0:T(8,128)(2,1)}) %all-gather.5.cloned.1.call-update) | async-done | bytes 2097168 | tf_op jit(solution)/shard_map/all_gather | solution.py:135
  65.4 2.3 %fusion.38 = f32[64,2048]{1,0:T(8,128)S(1)} fusion(bf16[2048,512]{1,0:T(8,128)(2,1)} %all-gather.5.cloned.1.call-done, bf16[4,8,8,128]{3,2,1,0:T(8,128)(2,1)S(1)} %fusion.15), kind=kOutput, calls=%fused_computation.52 | convolution fusion | flops 134217728 | bytes 2686976 | tf_op jit(solution)/shard_map/tc,oc->to/dot_general | solution.py:132
  67.7 0.0 copy-start.4
  67.8 1.5 collective-permute-start
  69.3 0.2 slice_reduce_fusion
  69.5 0.1 eq.88
  69.7 0.1 fusion.48
  69.8 0.1 reduce_sum.49
  69.9 3.6 %collective-permute-done = bf16[32,2048]{1,0:T(8,128)(2,1)S(1)} collective-permute-done((bf16[32,2048]{1,0:T(8,128)(2,1)S(1)}, bf16[32,2048]{1,0:T(8,128)(2,1)S(1)}, u32[]{:S(2)}, u32[]{:S(2)}) %collective-permute-start) | collective-permute-done | bytes 131104 | tf_op jit(solution)/shard_map/ppermute | solution.py:46
  73.5 0.0 copy-done.2
  73.5 0.2 fusion.20
  73.7 0.0 copy-done.3
  73.7 0.1 fusion.22
  73.8 1.5 collective-permute-start.1
  75.3 0.1 copy.50
  75.4 0.0 copy-done.4
  75.4 0.1 convert_reduce_fusion
  75.6 3.3 %collective-permute-done.1 = bf16[32,2048]{1,0:T(8,128)(2,1)S(1)} collective-permute-done((bf16[32,2048]{1,0:T(8,128)(2,1)S(1)}, bf16[32,2048]{1,0:T(8,128)(2,1)S(1)}, u32[]{:S(2)}, u32[]{:S(2)}) %collective-permute-start.1) | collective-permute-done | bytes 131104 | tf_op jit(solution)/shard_map/ppermute | solution.py:46
  78.8 0.6 convolution_convert_fusion.1
  79.4 0.0 copy-start.5
  79.4 41.0 %all_to_all.10 = bf16[8,48,2048]{2,1,0:T(8,128)(2,1)S(1)} all-to-all(bf16[8,48,2048]{2,1,0:T(8,128)(2,1)S(1)} %bitcast.73), channel_id=1, replica_groups=mesh['req'=2,'ctx'=8,'exp'=2] {'ctx'}, dimensions={0} | all-to-all | bytes 3145728 | tf_op jit(solution)/shard_map/all_to_all | solution.py:150
  120.4 0.0 copy-done.5
  120.4 0.0 copy-start.6
  120.4 0.9 fusion.3
  121.3 0.4 copy-done.6
  121.8 0.9 fusion.10
  122.7 0.2 copy.51
  122.9 0.0 copy-done
  122.9 2.1 %convolution_convert_fusion = bf16[8,48,2048]{2,1,0:T(8,128)(2,1)} fusion(bf16[8,48,352]{2,1,0:T(8,128)(2,1)S(1)} %bitcast.77, bf16[1,352,2048]{2,1,0:T(8,128)(2,1)S(1)} %copy-done), kind=kOutput, calls=%fused_computation | convolution fusion | flops 554434560 | bytes 3284992 | tf_op jit(solution)/shard_map/dot_general | solution.py:42
  125.1 3.6 %all-to-all-start.1 = ((bf16[8,48,2048]{2,1,0:T(8,128)(2,1)}), bf16[8,48,2048]{2,1,0:T(8,128)(2,1)S(1)}, u32[]{:S(2)}, u32[]{:S(2)}) async-start(bf16[8,48,2048]{2,1,0:T(8,128)(2,1)} %convolution_convert_fusion), calls=%async_computation.1 | async-start | bytes 3145728 | tf_op jit(solution)/shard_map/all_to_all | solution.py:156
  128.7 1.9 %fusion.17 = bf16[1,64,512]{2,1,0:T(8,128)(2,1)} fusion(s32[512]{0:T(512)S(1)} %fusion.56, s32[64]{0:T(128)S(1)} %iota_add_fusion, bf16[512,1024]{1,0:T(8,128)(2,1)} %all-gather.3.cloned.1.call-done), kind=kOutput, calls=%fused_computation.19 | convolution fusion | flops 33619968 | bytes 592128 | tf_op jit(solution)/shard_map/dot_general | solution.py:109
  130.6 35.8 %all-to-all-done.1 = bf16[8,48,2048]{2,1,0:T(8,128)(2,1)S(1)} async-done(((bf16[8,48,2048]{2,1,0:T(8,128)(2,1)}), bf16[8,48,2048]{2,1,0:T(8,128)(2,1)S(1)}, u32[]{:S(2)}, u32[]{:S(2)}) %all-to-all-start.1) | async-done | bytes 1572896 | tf_op jit(solution)/shard_map/all_to_all | solution.py:156
  166.4 0.0 copy-start.1
  166.4 0.9 fusion.73
  167.3 1.5 collective-permute-start.2
  168.8 0.0 copy-done.1
  168.8 0.9 fusion.16
  169.7 2.7 %collective-permute-done.2 = bf16[32,2048]{1,0:T(8,128)(2,1)S(1)} collective-permute-done((bf16[32,2048]{1,0:T(8,128)(2,1)S(1)}, bf16[32,2048]{1,0:T(8,128)(2,1)S(1)}, u32[]{:S(2)}, u32[]{:S(2)}) %collective-permute-start.2) | collective-permute-done | bytes 131104 | tf_op jit(solution)/shard_map/ppermute | solution.py:46
  172.4 0.7 fusion.37
  (12 shorter events, 0.2 us)
Async XLA Ops:
  7.2 115.8 %copy-start = (bf16[1,352,2048]{2,1,0:T(8,128)(2,1)S(1)}, bf16[1,352,2048]{2,1,0:T(8,128)(2,1)}, u32[]{:S(2)}) copy-start(bf16[1,352,2048]{2,1,0:T(8,128)(2,1)} %param.20) | copy-start | bytes 4325380
  7.2 27.9 %all-gather.3.cloned.1.call-start = ((), (), s32[]{:S(2)}) async-start(), calls=%async_computation.2 | async-start | bytes 1179648 | tf_op jit(solution)/shard_map/all_gather | solution.py:102
  8.9 56.5 %all-gather.5.cloned.1.call-start = ((), (), s32[]{:S(2)}) async-start(), calls=%async_computation.3 | async-start | bytes 2359296 | tf_op jit(solution)/shard_map/all_gather | solution.py:135
  37.7 35.8 %copy-start.2 = (bf16[1,32,2048]{2,1,0:T(8,128)(2,1)S(1)}, bf16[1,32,2048]{2,1,0:T(8,128)(2,1)}, u32[]{:S(2)}) copy-start(bf16[1,32,2048]{2,1,0:T(8,128)(2,1)} %param.15) | copy-start | bytes 393220
  37.7 36.0 %copy-start.3 = (f32[2048]{0:T(1024)S(1)}, f32[2048]{0:T(1024)}, u32[]{:S(2)}) copy-start(f32[2048]{0:T(1024)} %param.17) | copy-start | bytes 24580
  67.7 7.7 %copy-start.4 = (f32[1,64,4]{1,2,0:T(4,128)S(1)}, f32[1,64,4]{1,2,0:T(4,128)}, u32[]{:S(2)}) copy-start(f32[1,64,4]{1,2,0:T(4,128)} %param.22) | copy-start | bytes 3076
  67.8 5.7 %collective-permute-start = (bf16[32,2048]{1,0:T(8,128)(2,1)S(1)}, bf16[32,2048]{1,0:T(8,128)(2,1)S(1)}, u32[]{:S(2)}, u32[]{:S(2)}) collective-permute-start(bf16[32,2048]{1,0:T(8,128)(2,1)S(1)} %select_convert_fusion.1), channel_id=1, source_target_pairs={{0,1},{1,0},{2,3},{3,2},{4,5},{5,4},{6,7},{7,6},{8,9},{9,8},{10,11... | collective-permute-start | bytes 393224 | tf_op jit(solution)/shard_map/ppermute | solution.py:46
  73.8 5.0 %collective-permute-start.1 = (bf16[32,2048]{1,0:T(8,128)(2,1)S(1)}, bf16[32,2048]{1,0:T(8,128)(2,1)S(1)}, u32[]{:S(2)}, u32[]{:S(2)}) collective-permute-start(bf16[32,2048]{1,0:T(8,128)(2,1)S(1)} %fusion.22), channel_id=1, source_target_pairs={{0,1},{1,0},{2,3},{3,2},{4,5},{5,4},{6,7},{7,6},{8,9},{9,8},{10,11... | collective-permute-start | bytes 393224 | tf_op jit(solution)/shard_map/ppermute | solution.py:46
  79.4 41.0 %copy-start.5 = (bf16[1,2048,352]{1,2,0:T(8,128)(2,1)S(1)}, bf16[1,2048,352]{1,2,0:T(8,128)(2,1)}, u32[]{:S(2)}) copy-start(bf16[1,2048,352]{1,2,0:T(8,128)(2,1)} %param.18) | copy-start | bytes 4325380
  120.4 1.4 copy-start.6
  125.1 41.3 %all-to-all-start.1 = ((bf16[8,48,2048]{2,1,0:T(8,128)(2,1)}), bf16[8,48,2048]{2,1,0:T(8,128)(2,1)S(1)}, u32[]{:S(2)}, u32[]{:S(2)}) async-start(bf16[8,48,2048]{2,1,0:T(8,128)(2,1)} %convolution_convert_fusion), calls=%async_computation.1 | async-start | bytes 3145728 | tf_op jit(solution)/shard_map/all_to_all | solution.py:156
  166.4 2.4 %copy-start.1 = (bf16[512,1024]{1,0:T(8,128)(2,1)S(1)}, bf16[512,1024]{1,0:T(8,128)(2,1)}, u32[]{:S(2)}) copy-start(bf16[512,1024]{1,0:T(8,128)(2,1)} %all-gather.3.cloned.1.call-done) | copy-start | bytes 3145732
  167.3 5.1 %collective-permute-start.2 = (bf16[32,2048]{1,0:T(8,128)(2,1)S(1)}, bf16[32,2048]{1,0:T(8,128)(2,1)S(1)}, u32[]{:S(2)}, u32[]{:S(2)}) collective-permute-start(bf16[32,2048]{1,0:T(8,128)(2,1)S(1)} %select_convert_fusion), channel_id=1, source_target_pairs={{0,1},{1,0},{2,3},{3,2},{4,5},{5,4},{6,7},{7,6},{8,9},{9,8},{10,11... | collective-permute-start | bytes 393224 | tf_op jit(solution)/shard_map/ppermute | solution.py:46
Sparse Core Ops, SparseCore 0:
  10.2 24.8 all-gather.2
  36.6 28.7 all-gather.4
where the time goes:
time: 180 us
  waiting for transfers between devices  96.1 us (53%)
  blocking collectives  41 us (23%)
  between operations  14.9 us (8%)
  matrix products  11.2 us (6%)
  starting transfers between devices  8.24 us (5%)
  local copies, waits for them, and re-layouts  4.62 us (3%)
  other arithmetic  3.95 us (2%)
    all_to_all x1, blocking collectives, local(): lax.all_to_all(send_rows, 'ctx', split_axis=0, concat_axis=0, tiled=True)  41 us
    all_to_all x1, waiting for transfers between devices, local(): lax.all_to_all(produced.astype(jnp.bfloat16), 'ctx', split_axis=0, concat...  35.8 us
    all_gather x1, waiting for transfers between devices, local(): lax.all_gather(out_weight, 'ctx', axis=0, tiled=True)  27.7 us
    all_gather x1, waiting for transfers between devices, local(): kv_all = lax.all_gather(kv_here, 'ctx', axis=0, tiled=True)  22.2 us
    ppermute x3, waiting for transfers between devices, exp_swap(): return lax.ppermute(x, 'exp', perm=[(0, 1), (1, 0)])  9.58 us
    ppermute x3, starting transfers between devices, exp_swap(): return lax.ppermute(x, 'exp', perm=[(0, 1), (1, 0)])  4.58 us
  transfers between devices with their start and end apart: 6, of which 6 were waited for; matrix products, arithmetic and copies ran while one was open for 5% of the time, Pallas kernels for 0%

commit v1 on v0

--- a/solution.py
+++ b/solution.py
@@ -8,6 +8,25 @@
 TOP = 4
 EPS = 1e-06
 NEG = -1e30
+
+
+def in_order(pieces, dim):
+    shape = list(pieces.shape[1:])
+    shape[dim] *= pieces.shape[0]
+    return jnp.moveaxis(pieces, 0, dim).reshape(shape)
+
+
+def doubled(x, axis):
+    size, position = (lax.axis_size(axis), lax.axis_index(axis))
+    blocks, apart = (x[None], 1)
+    while apart < size:
+        partner_block = lax.ppermute(blocks, axis, [(i, i ^ apart) for i in range(size)])
+        low = position & apart == 0
+        blocks = jnp.concatenate(
+            [jnp.where(low, blocks, partner_block), jnp.where(low, partner_block, blocks)]
+        )
+        apart *= 2
+    return blocks
 
 
 def row_positions(row_ids, half_block, n_groups):
@@ -99,7 +118,7 @@
     query_three = query_states[0].reshape(tok_here, heads_dev, HD)
     run_max = jnp.full((heads_dev, tok_here), NEG, jnp.float32)
     kv_here = jnp.concatenate([key_states[0], value_states[0]], axis=1)
-    kv_all = lax.all_gather(kv_here, "ctx", axis=0, tiled=True)
+    kv_all = in_order(doubled(kv_here, "ctx"), 0)
     key_two = kv_all[:, :feat_width]
     value_two = kv_all[:, feat_width:]
     row_count = key_two.shape[0]

time: 180 us -> 180 us (level)
  starting transfers between devices: 8.24 us -> 14.5 us
  waiting for transfers between devices: 96.1 us -> 90.9 us
    ppermute x0 -> x3, waiting for transfers between devices: none -> 45.1 us  [doubled(): lax.ppermute(blocks, axis, [(i, i ^ apart) for i in range(size)])]
    all_gather x1, waiting for transfers between devices: 27.7 us -> 0.02 us  [local(): lax.all_gather(out_weight, 'ctx', axis=0, tiled=True)]
    all_gather x1 -> x0, waiting for transfers between devices: 22.2 us -> none  [local(): kv_all = lax.all_gather(kv_here, 'ctx', axis=0, tiled=True)]
    ppermute x0 -> x3, starting transfers between devices: none -> 6.33 us  [doubled(): lax.ppermute(blocks, axis, [(i, i ^ apart) for i in range(size)])]
  transfers between devices with their start and end apart: 6 -> 8, of which waited for: 6 -> 7; matrix products, arithmetic and copies ran while one was open for 5% -> 4% of each run, Pallas kernels for 0% -> 0%
where the time goes in v1:
time: 180 us; the launch traced here: 179 us
  waiting for transfers between devices  90.9 us (50%)
  blocking collectives  40.4 us (22%)
  between operations  15 us (8%)
  starting transfers between devices  14.5 us (8%)
  matrix products  11.3 us (6%)
  other arithmetic  4.4 us (2%)
  local copies, waits for them, and re-layouts  2.91 us (2%)
    ppermute x3, waiting for transfers between devices, doubled(): lax.ppermute(blocks, axis, [(i, i ^ apart) for i in range(size)])  45.1 us
    all_to_all x1, blocking collectives, local(): lax.all_to_all(send_rows, 'ctx', split_axis=0, concat_axis=0, tiled=True)  40.4 us
    all_to_all x1, waiting for transfers between devices, local(): lax.all_to_all(produced.astype(jnp.bfloat16), 'ctx', split_axis=0, concat...  35.8 us
    ppermute x3, waiting for transfers between devices, exp_swap(): return lax.ppermute(x, 'exp', perm=[(0, 1), (1, 0)])  9.3 us
    ppermute x3, starting transfers between devices, doubled(): lax.ppermute(blocks, axis, [(i, i ^ apart) for i in range(size)])  6.33 us
    ppermute x3, starting transfers between devices, exp_swap(): return lax.ppermute(x, 'exp', perm=[(0, 1), (1, 0)])  4.52 us
  transfers between devices with their start and end apart: 8, of which 7 were waited for; matrix products, arithmetic and copies ran while one was open for 4% of the time, Pallas kernels for 0%

profile of v1, /device:TPU:0, one launch (start us, length us, event | category | flops | bytes accessed | tf_op | source)
XLA Modules:
  0.0 179.3 jit_solution(166846658654228128)
XLA Ops:
  7.2 0.0 copy-start
  7.2 0.0 copy-start.4
  7.2 0.0 copy-start.7
  7.2 0.0 all-gather.2.cloned.1.call-start
  7.2 0.7 all-gather.2.cloned.1.call-update
  7.9 0.9 maximum_bitcast_fusion
  8.8 0.5 collective-permute-start
  9.3 1.0 collective-permute-done
  10.3 0.9 broadcast_select_fusion.5
  11.3 3.0 %collective-permute-start.1 = (bf16[2,64,1024]{2,1,0:T(8,128)(2,1)S(1)}, bf16[2,64,1024]{2,1,0:T(8,128)(2,1)S(1)}, u32[]{:S(2)}, u32[]{:S(2)}) collective-permute-start(bf16[2,64,1024]{2,1,0:T(8,128)(2,1)S(1)} %pad_maximum_fusion.2), channel_id=1, source_target_pairs={{0,4},{2,6},{4,0},{6,2},{8,12},{10,14},{12,8},{14,10},{1,5},{3,7},... | collective-permute-start | bytes 786440 | tf_op jit(solution)/shard_map/ppermute | solution.py:23
  14.9 0.0 copy-done.4
  15.0 0.0 copy-done.7
  15.0 0.1 copy.46
  15.1 0.1 eq.104
  15.2 0.6 reduce-window.6
  15.8 5.1 %collective-permute-done.1 = bf16[2,64,1024]{2,1,0:T(8,128)(2,1)S(1)} collective-permute-done((bf16[2,64,1024]{2,1,0:T(8,128)(2,1)S(1)}, bf16[2,64,1024]{2,1,0:T(8,128)(2,1)S(1)}, u32[]{:S(2)}, u32[]{:S(2)}) %collective-permute-start.1) | collective-permute-done | bytes 262176 | tf_op jit(solution)/shard_map/ppermute | solution.py:23
  21.0 2.8 %collective-permute-start.2 = (bf16[4,64,1024]{2,1,0:T(8,128)(2,1)S(1)}, bf16[4,64,1024]{2,1,0:T(8,128)(2,1)S(1)}, u32[]{:S(2)}, u32[]{:S(2)}) collective-permute-start(bf16[4,64,1024]{2,1,0:T(8,128)(2,1)S(1)} %pad_maximum_fusion.1), channel_id=1, source_target_pairs={{0,8},{2,10},{4,12},{6,14},{8,0},{10,2},{12,4},{14,6},{1,9},{3,11}... | collective-permute-start | bytes 1572872 | tf_op jit(solution)/shard_map/ppermute | solution.py:23
  23.9 0.1 compare_and_fusion
  24.0 39.0 %collective-permute-done.2 = bf16[4,64,1024]{2,1,0:T(8,128)(2,1)S(1)} collective-permute-done((bf16[4,64,1024]{2,1,0:T(8,128)(2,1)S(1)}, bf16[4,64,1024]{2,1,0:T(8,128)(2,1)S(1)}, u32[]{:S(2)}, u32[]{:S(2)}) %collective-permute-start.2) | collective-permute-done | bytes 524320 | tf_op jit(solution)/shard_map/ppermute | solution.py:23
  63.0 0.1 broadcast_select_fusion.1
  63.1 0.1 pad_maximum_fusion
  63.2 0.0 copy-start.1
  63.2 1.0 copy-done.1
  64.2 0.1 fusion.71
  64.2 0.2 copy.40
  64.5 0.2 copy.43
  64.7 0.3 fusion.72
  65.0 0.2 fusion.18
  65.2 0.3 fusion.15
  65.6 0.0 copy-start.3
  65.6 0.0 copy-start.5
  65.6 0.0 all-gather.2.cloned.1.call-done
  65.6 2.4 %fusion.38 = f32[64,2048]{1,0:T(8,128)S(1)} fusion(bf16[2048,512]{1,0:T(8,128)(2,1)} %all-gather.2.cloned.1.call-done, bf16[4,8,8,128]{3,2,1,0:T(8,128)(2,1)S(1)} %fusion.15), kind=kOutput, calls=%fused_computation.61 | convolution fusion | flops 134217728 | bytes 2686976 | tf_op jit(solution)/shard_map/tc,oc->to/dot_general | solution.py:151
  68.0 0.0 copy-start.6
  68.0 1.5 collective-permute-start.3
  69.6 0.2 slice_reduce_fusion
  69.8 0.1 eq.100
  70.0 0.1 fusion.48
  70.0 0.1 reduce_sum.49
  70.2 3.3 %collective-permute-done.3 = bf16[32,2048]{1,0:T(8,128)(2,1)S(1)} collective-permute-done((bf16[32,2048]{1,0:T(8,128)(2,1)S(1)}, bf16[32,2048]{1,0:T(8,128)(2,1)S(1)}, u32[]{:S(2)}, u32[]{:S(2)}) %collective-permute-start.3) | collective-permute-done | bytes 131104 | tf_op jit(solution)/shard_map/ppermute | solution.py:65
  73.4 0.2 fusion.20
  73.6 0.1 fusion.22
  73.7 1.5 collective-permute-start.4
  75.2 0.1 copy.49
  75.3 0.0 copy-done.6
  75.3 0.1 convert_reduce_fusion
  75.4 3.3 %collective-permute-done.4 = bf16[32,2048]{1,0:T(8,128)(2,1)S(1)} collective-permute-done((bf16[32,2048]{1,0:T(8,128)(2,1)S(1)}, bf16[32,2048]{1,0:T(8,128)(2,1)S(1)}, u32[]{:S(2)}, u32[]{:S(2)}) %collective-permute-start.4) | collective-permute-done | bytes 131104 | tf_op jit(solution)/shard_map/ppermute | solution.py:65
  78.7 0.6 convolution_convert_fusion.1
  79.3 0.0 copy-start.8
  79.4 40.4 %all_to_all.10 = bf16[8,48,2048]{2,1,0:T(8,128)(2,1)S(1)} all-to-all(bf16[8,48,2048]{2,1,0:T(8,128)(2,1)S(1)} %bitcast.80), channel_id=1, replica_groups=mesh['req'=2,'ctx'=8,'exp'=2] {'ctx'}, dimensions={0} | all-to-all | bytes 3145728 | tf_op jit(solution)/shard_map/all_to_all | solution.py:169
  119.7 0.9 fusion.3
  120.7 0.4 copy-done.9
  121.1 0.9 fusion.10
  122.1 0.2 copy.50
  122.3 0.0 copy-done
  122.3 2.1 %convolution_convert_fusion = bf16[8,48,2048]{2,1,0:T(8,128)(2,1)} fusion(bf16[8,48,352]{2,1,0:T(8,128)(2,1)S(1)} %bitcast.87, bf16[1,352,2048]{2,1,0:T(8,128)(2,1)S(1)} %copy-done), kind=kOutput, calls=%fused_computation | convolution fusion | flops 554434560 | bytes 3284992 | tf_op jit(solution)/shard_map/dot_general | solution.py:61
  124.4 3.6 %all-to-all-start.1 = ((bf16[8,48,2048]{2,1,0:T(8,128)(2,1)}), bf16[8,48,2048]{2,1,0:T(8,128)(2,1)S(1)}, u32[]{:S(2)}, u32[]{:S(2)}) async-start(bf16[8,48,2048]{2,1,0:T(8,128)(2,1)} %convolution_convert_fusion), calls=%async_computation.1 | async-start | bytes 3145728 | tf_op jit(solution)/shard_map/all_to_all | solution.py:175
  128.0 1.9 %fusion.16 = bf16[1,64,512]{2,1,0:T(8,128)(2,1)} fusion(s32[512]{0:T(512)S(1)} %fusion.56, s32[64]{0:T(128)S(1)} %iota_add_fusion, bf16[512,1024]{1,0:T(8,128)(2,1)} %bitcast.82), kind=kOutput, calls=%fused_computation.18 | convolution fusion | flops 33619968 | bytes 592128 | tf_op jit(solution)/shard_map/dot_general | solution.py:127
  129.9 35.8 %all-to-all-done.1 = bf16[8,48,2048]{2,1,0:T(8,128)(2,1)S(1)} async-done(((bf16[8,48,2048]{2,1,0:T(8,128)(2,1)}), bf16[8,48,2048]{2,1,0:T(8,128)(2,1)S(1)}, u32[]{:S(2)}, u32[]{:S(2)}) %all-to-all-start.1) | async-done | bytes 1572896 | tf_op jit(solution)/shard_map/all_to_all | solution.py:175
  165.8 0.9 fusion.73
  166.7 1.5 collective-permute-start.5
  168.2 0.9 fusion.17
  169.1 2.7 %collective-permute-done.5 = bf16[32,2048]{1,0:T(8,128)(2,1)S(1)} collective-permute-done((bf16[32,2048]{1,0:T(8,128)(2,1)S(1)}, bf16[32,2048]{1,0:T(8,128)(2,1)S(1)}, u32[]{:S(2)}, u32[]{:S(2)}) %collective-permute-start.5) | collective-permute-done | bytes 131104 | tf_op jit(solution)/shard_map/ppermute | solution.py:65
  171.8 0.7 fusion.37
  (22 shorter events, 0.3 us)
Async XLA Ops:
  7.2 115.1 %copy-start = (bf16[1,352,2048]{2,1,0:T(8,128)(2,1)S(1)}, bf16[1,352,2048]{2,1,0:T(8,128)(2,1)}, u32[]{:S(2)}) copy-start(bf16[1,352,2048]{2,1,0:T(8,128)(2,1)} %param.20) | copy-start | bytes 4325380
  7.2 7.8 %copy-start.4 = (bf16[1,64,512]{2,1,0:T(8,128)(2,1)S(1)}, bf16[1,64,512]{2,1,0:T(8,128)(2,1)}, u32[]{:S(2)}) copy-start(bf16[1,64,512]{2,1,0:T(8,128)(2,1)} %param.12) | copy-start | bytes 196612
  7.2 7.8 %copy-start.7 = (s32[1,64,4]{1,2,0:T(4,128)S(1)}, s32[1,64,4]{1,2,0:T(4,128)}, u32[]{:S(2)}) copy-start(s32[1,64,4]{1,2,0:T(4,128)} %param.21) | copy-start | bytes 3076
  7.2 58.4 %all-gather.2.cloned.1.call-start = ((), (), s32[]{:S(2)}) async-start(), calls=%async_computation.2 | async-start | bytes 2359296 | tf_op jit(solution)/shard_map/all_gather | solution.py:154
  8.8 1.5 collective-permute-start
  11.3 9.6 %collective-permute-start.1 = (bf16[2,64,1024]{2,1,0:T(8,128)(2,1)S(1)}, bf16[2,64,1024]{2,1,0:T(8,128)(2,1)S(1)}, u32[]{:S(2)}, u32[]{:S(2)}) collective-permute-start(bf16[2,64,1024]{2,1,0:T(8,128)(2,1)S(1)} %pad_maximum_fusion.2), channel_id=1, source_target_pairs={{0,4},{2,6},{4,0},{6,2},{8,12},{10,14},{12,8},{14,10},{1,5},{3,7},... | collective-permute-start | bytes 786440 | tf_op jit(solution)/shard_map/ppermute | solution.py:23
  21.0 42.0 %collective-permute-start.2 = (bf16[4,64,1024]{2,1,0:T(8,128)(2,1)S(1)}, bf16[4,64,1024]{2,1,0:T(8,128)(2,1)S(1)}, u32[]{:S(2)}, u32[]{:S(2)}) collective-permute-start(bf16[4,64,1024]{2,1,0:T(8,128)(2,1)S(1)} %pad_maximum_fusion.1), channel_id=1, source_target_pairs={{0,8},{2,10},{4,12},{6,14},{8,0},{10,2},{12,4},{14,6},{1,9},{3,11}... | collective-permute-start | bytes 1572872 | tf_op jit(solution)/shard_map/ppermute | solution.py:23
  63.2 1.0 copy-start.1
  65.6 7.8 %copy-start.3 = (bf16[1,32,2048]{2,1,0:T(8,128)(2,1)S(1)}, bf16[1,32,2048]{2,1,0:T(8,128)(2,1)}, u32[]{:S(2)}) copy-start(bf16[1,32,2048]{2,1,0:T(8,128)(2,1)} %param.15) | copy-start | bytes 393220
  65.6 8.0 %copy-start.5 = (f32[2048]{0:T(1024)S(1)}, f32[2048]{0:T(1024)}, u32[]{:S(2)}) copy-start(f32[2048]{0:T(1024)} %param.17) | copy-start | bytes 24580
  68.0 7.3 %copy-start.6 = (f32[1,64,4]{1,2,0:T(4,128)S(1)}, f32[1,64,4]{1,2,0:T(4,128)}, u32[]{:S(2)}) copy-start(f32[1,64,4]{1,2,0:T(4,128)} %param.22) | copy-start | bytes 3076
  68.0 5.4 %collective-permute-start.3 = (bf16[32,2048]{1,0:T(8,128)(2,1)S(1)}, bf16[32,2048]{1,0:T(8,128)(2,1)S(1)}, u32[]{:S(2)}, u32[]{:S(2)}) collective-permute-start(bf16[32,2048]{1,0:T(8,128)(2,1)S(1)} %select_convert_fusion.1), channel_id=1, source_target_pairs={{0,1},{1,0},{2,3},{3,2},{4,5},{5,4},{6,7},{7,6},{8,9},{9,8},{10,11... | collective-permute-start | bytes 393224 | tf_op jit(solution)/shard_map/ppermute | solution.py:65
  73.7 5.0 %collective-permute-start.4 = (bf16[32,2048]{1,0:T(8,128)(2,1)S(1)}, bf16[32,2048]{1,0:T(8,128)(2,1)S(1)}, u32[]{:S(2)}, u32[]{:S(2)}) collective-permute-start(bf16[32,2048]{1,0:T(8,128)(2,1)S(1)} %fusion.22), channel_id=1, source_target_pairs={{0,1},{1,0},{2,3},{3,2},{4,5},{5,4},{6,7},{7,6},{8,9},{9,8},{10,11... | collective-permute-start | bytes 393224 | tf_op jit(solution)/shard_map/ppermute | solution.py:65
  79.3 40.4 %copy-start.8 = (bf16[1,2048,352]{1,2,0:T(8,128)(2,1)S(1)}, bf16[1,2048,352]{1,2,0:T(8,128)(2,1)}, u32[]{:S(2)}) copy-start(bf16[1,2048,352]{1,2,0:T(8,128)(2,1)} %param.18) | copy-start | bytes 4325380
  119.7 1.4 copy-start.9
  124.4 41.3 %all-to-all-start.1 = ((bf16[8,48,2048]{2,1,0:T(8,128)(2,1)}), bf16[8,48,2048]{2,1,0:T(8,128)(2,1)S(1)}, u32[]{:S(2)}, u32[]{:S(2)}) async-start(bf16[8,48,2048]{2,1,0:T(8,128)(2,1)} %convolution_convert_fusion), calls=%async_computation.1 | async-start | bytes 3145728 | tf_op jit(solution)/shard_map/all_to_all | solution.py:175
  165.8 2.4 %copy-start.2 = (bf16[8,64,1024]{2,1,0:T(8,128)(2,1)S(1)}, bf16[8,64,1024]{2,1,0:T(8,128)(2,1)}, u32[]{:S(2)}) copy-start(bf16[8,64,1024]{2,1,0:T(8,128)(2,1)} %copy-done.1) | copy-start | bytes 3145732
  166.7 5.1 %collective-permute-start.5 = (bf16[32,2048]{1,0:T(8,128)(2,1)S(1)}, bf16[32,2048]{1,0:T(8,128)(2,1)S(1)}, u32[]{:S(2)}, u32[]{:S(2)}) collective-permute-start(bf16[32,2048]{1,0:T(8,128)(2,1)S(1)} %select_convert_fusion), channel_id=1, source_target_pairs={{0,1},{1,0},{2,3},{3,2},{4,5},{5,4},{6,7},{7,6},{8,9},{9,8},{10,11... | collective-permute-start | bytes 393224 | tf_op jit(solution)/shard_map/ppermute | solution.py:65
Sparse Core Ops, SparseCore 0:
  9.6 51.8 all-gather.1
